TPU v7x, 128 devices: a whole 4x4x4 slice. The times are simulated.
128 devices in a mesh: dof: 32 (over x, z, core), snap: 4 (over y).
Axes of the slice: x: 4, y: 4, z: 4, core: 2. Of those that a mesh axis runs over, the one named last changes fastest.
Arguments:
- snapshots: bfloat16 [131072, 1024], P('dof', 'snap')
- lengths: int32 [16], replicated, may hold values from 16 to 64, as said below
- start_block: float32 [1024, 128], replicated, may hold values from -6 to 6
Outputs:
- pod_modes: float32 [131072, 128], P(('dof', 'snap'))
- r_factor: float32 [1024, 1024], replicated
Inputs may be any that keep to these rules, and one draw needn't show every extreme that they name: `lengths`: some passage has all 64 steps active and some passage only a quarter of them.
All inputs are finite; a program needn't handle non-finite values.
Results may differ from a plain program's by a relative error of at most 0.0003.
Values may be sent and summed in bfloat16 or wider, within the bound.
No kernel may reach another device: no remote copies, remote signals or barrier semaphores. Data moves between devices by JAX's collectives and lax.ppermute only.
A program may use at most 128 MiB of HBM per device.

v0:
```python
import jax
import jax.numpy as jnp
from jax import lax
from jax.sharding import PartitionSpec as P

STEPS = 64
ITERS = 3
PASSES = 16
TILE = 128


def pack_upper(rows):
    width = rows.shape[1]
    pieces = []
    for i in range(width // TILE):
        lhs = rows[:, i * TILE : (i + 1) * TILE]
        rhs = rows[:, i * TILE :]
        pieces.append(
            lax.dot_general(lhs, rhs, (((0,), (0,)), ((), ())), preferred_element_type=jnp.float32)
        )
    return jnp.concatenate(pieces, axis=1)


def unpack_upper(packed, width):
    blocks = width // TILE
    upper_rows = []
    offset = 0
    for i in range(blocks):
        w = width - i * TILE
        piece = packed[:, offset : offset + w]
        offset += w
        upper_rows.append(jnp.pad(piece, ((0, 0), (i * TILE, 0))))
    upper = jnp.concatenate(upper_rows, axis=0)
    r = lax.broadcasted_iota(jnp.int32, (width, width), 0) // TILE
    c = lax.broadcasted_iota(jnp.int32, (width, width), 1) // TILE
    return jnp.where(r <= c, upper, upper.T)


def body(snapshots, lengths, start_block):
    rows = lax.all_to_all(snapshots, "snap", 0, 1, tiled=True)
    width = rows.shape[1]
    col_length = jnp.repeat(lengths, STEPS, total_repeat_length=width)
    columns = jnp.arange(width, dtype=jnp.int32)
    active = columns % STEPS < col_length
    masked = jnp.where(active[None, :], rows, jnp.zeros_like(rows))
    row_count = snapshots.shape[0] * lax.axis_size("dof")
    packed = lax.psum(pack_upper(masked), ("dof", "snap"))
    gram_sum = unpack_upper(packed, width)
    shifted = gram_sum / jnp.float32(row_count) + 0.05 * jnp.eye(width, dtype=jnp.float32)
    upper_factor = lax.linalg.cholesky(shifted, symmetrize_input=False).T
    contract = (((0,), (0,)), ((), ()))
    subspace = start_block
    for sweep in range(ITERS):
        image = jnp.dot(
            shifted, subspace, precision=lax.Precision.HIGHEST, preferred_element_type=jnp.float32
        )
        correlation = lax.dot_general(
            image,
            image,
            contract,
            precision=lax.Precision.HIGHEST,
            preferred_element_type=jnp.float32,
        )
        lower_factor = jnp.linalg.cholesky(correlation)
        subspace = lax.linalg.triangular_solve(
            lower_factor, image, left_side=False, lower=True, transpose_a=True
        )
    pod_modes = jnp.dot(
        masked.astype(jnp.float32),
        subspace,
        precision=lax.Precision.HIGHEST,
        preferred_element_type=jnp.float32,
    )
    return (pod_modes, upper_factor)


def solution(mesh):
    placed = (P("dof", "snap"), P(), P())
    return jax.shard_map(
        body, mesh=mesh, in_specs=placed, out_specs=(P(("dof", "snap"), None), P()), check_vma=False
    )
```

profile of v0, /device:TPU:1, one launch (start us, length us, event | category | flops | bytes accessed | tf_op | source)
XLA Modules:
  0.0 540.3 jit_solution(2373709611297239090)
XLA Ops:
  7.2 5.2 all-to-all-start
  13.2 4.4 compare_select_fusion.1
  17.7 5.7 %fusion.98 = pred[1024]{0:T(1024)(128)(4,1)S(1)} fusion(pred[1024]{0:T(1024)(128)(4,1)S(1)} %get-tuple-element.30, pred[1024]{0:T(1024)(128)(4,1)S(1)} %get-tuple-element.29, pred[1024]{0:T(1024)(128)(4,1)S(1)} %get-tuple-element.28, pred[1024]{0:T(1024)(128)(4,1)S(1)} %get-tuple-element.27, pred[1024]{0:T(1024)(128)(4,1)S(1)} %get-tuple-element.26, ...), kind=kLoop, calls=%fused_computation.159 | loop fusion | flops 25600 | bytes 18500 | tf_op jit(solution)/shard_map/lt | solution.py:44
  23.4 14.4 %all-to-all-done = bf16[4,1024,256]{2,1,0:T(8,128)(2,1)S(1)} async-done(((bf16[4,1024,256]{2,1,0:T(8,128)(2,1)}), bf16[4,1024,256]{2,1,0:T(8,128)(2,1)S(1)}, u32[]{:S(2)}, u32[]{:S(2)}) %all-to-all-start) | async-done | bytes 2097184 | tf_op jit(solution)/shard_map/all_to_all | solution.py:40
  37.8 2.4 copy.29
  40.1 1.8 bitcast_select_fusion.1
  42.0 1.5 convolution_dynamic-update-slice_fusion
  51.5 152.8 %all-reduce.10.cloned.1.call-done = f32[128,4608]{0,1:T(8,128)} async-done(((f32[128,4608]{0,1:T(8,128)}), f32[128,4608]{0,1:T(8,128)}) %all-reduce.10.cloned.1.call-update) | async-done | bytes 2359312 | tf_op jit(solution)/shard_map/psum | solution.py:47
  205.4 1.9 slice_dynamic-update-slice_fusion
  214.1 5.3 copy.37
  219.5 4.2 fusion.1
  223.7 2.0 copy-done.1
  225.7 11.7 %cholesky.247 = f32[128,128]{1,0:T(8,128)S(1)} custom-call(f32[128,128]{1,0:T(8,128)S(1)} %cholesky.667), custom_call_target="Cholesky" | custom-call | tf_op jit(solution)/shard_map/cholesky | solution.py:50
  238.1 9.8 %custom-call.49 = f32[1,128,128]{1,2,0:T(8,128)S(1)} custom-call(f32[1,128,128]{2,1,0:T(8,128)S(1)} %get-tuple-element.54), custom_call_target="InvertDiagBlocksLowerTriangular" | custom-call | tf_op jit(solution)/shard_map/cholesky | solution.py:50
  247.9 5.4 fusion.106
  254.5 11.7 %cholesky.636 = f32[128,128]{1,0:T(8,128)S(1)} custom-call(f32[128,128]{1,0:T(8,128)S(1)} %fusion.63), custom_call_target="Cholesky" | custom-call | tf_op jit(solution)/shard_map/jit(cholesky)/cholesky | solution.py:64
  267.5 9.8 %custom-call.58 = f32[1,128,128]{1,2,0:T(8,128)S(1)} custom-call(f32[1,128,128]{2,1,0:T(8,128)S(1)} %fusion.46), custom_call_target="InvertDiagBlocksLowerTriangular" | custom-call | tf_op jit(solution)/shard_map/triangular_solve/custom-call.16 | solution.py:65
  278.0 5.4 %fusion.108 = f32[1024,128]{1,0:T(8,128)S(1)} fusion(f32[1024,1024]{1,0:T(8,128)} %copy-done.1, f32[1024,128]{0,1:T(8,128)S(1)} %convolution_bitcast_fusion.2), kind=kOutput, calls=%fused_computation.192 | convolution fusion | flops 1610612736 | bytes 5242880 | tf_op jit(solution)/shard_map/dot_general | solution.py:54
  284.6 11.7 %cholesky.647 = f32[128,128]{1,0:T(8,128)S(1)} custom-call(f32[128,128]{1,0:T(8,128)S(1)} %fusion.61), custom_call_target="Cholesky" | custom-call | tf_op jit(solution)/shard_map/jit(cholesky)/cholesky | solution.py:64
  297.6 9.8 %custom-call.59 = f32[1,128,128]{1,2,0:T(8,128)S(1)} custom-call(f32[1,128,128]{2,1,0:T(8,128)S(1)} %fusion.47), custom_call_target="InvertDiagBlocksLowerTriangular" | custom-call | tf_op jit(solution)/shard_map/triangular_solve/custom-call.16 | solution.py:65
  308.1 5.6 %fusion.110 = f32[1024,128]{1,0:T(8,128)S(1)} fusion(f32[1024,1024]{1,0:T(8,128)} %copy-done.1, f32[1024,128]{0,1:T(8,128)S(1)} %convolution_bitcast_fusion.1), kind=kOutput, calls=%fused_computation.194 | convolution fusion | flops 1610612736 | bytes 5242880 | tf_op jit(solution)/shard_map/dot_general | solution.py:54
  314.8 11.7 %cholesky.658 = f32[128,128]{1,0:T(8,128)S(1)} custom-call(f32[128,128]{1,0:T(8,128)S(1)} %fusion.59), custom_call_target="Cholesky" | custom-call | tf_op jit(solution)/shard_map/jit(cholesky)/cholesky | solution.py:64
  327.9 9.8 %custom-call.60 = f32[1,128,128]{1,2,0:T(8,128)S(1)} custom-call(f32[1,128,128]{2,1,0:T(8,128)S(1)} %fusion.48), custom_call_target="InvertDiagBlocksLowerTriangular" | custom-call | tf_op jit(solution)/shard_map/triangular_solve/custom-call.16 | solution.py:65
  338.4 3.1 fusion.112
  341.5 2.5 cholesky.279
  343.9 2.4 constant_dynamic-update-slice_fusion.6
  346.3 1.5 convolution_subtract_fusion
  347.9 11.9 %cholesky.270 = f32[128,128]{1,0:T(8,128)S(1)} custom-call(f32[128,128]{1,0:T(8,128)S(1)} %cholesky.671), custom_call_target="Cholesky" | custom-call | tf_op jit(solution)/shard_map/cholesky | solution.py:50
  361.1 9.8 %custom-call.50 = f32[1,128,128]{1,2,0:T(8,128)S(1)} custom-call(f32[1,128,128]{2,1,0:T(8,128)S(1)} %get-tuple-element.51), custom_call_target="InvertDiagBlocksLowerTriangular" | custom-call | tf_op jit(solution)/shard_map/cholesky | solution.py:50
  372.2 2.1 convolution_subtract_fusion.1
  374.3 11.7 %cholesky.493 = f32[128,128]{1,0:T(8,128)S(1)} custom-call(f32[128,128]{1,0:T(8,128)S(1)} %cholesky.676), custom_call_target="Cholesky" | custom-call | tf_op jit(solution)/shard_map/cholesky | solution.py:50
  387.3 10.0 %custom-call.51 = f32[1,128,128]{1,2,0:T(8,128)S(1)} custom-call(f32[1,128,128]{2,1,0:T(8,128)S(1)} %get-tuple-element.48), custom_call_target="InvertDiagBlocksLowerTriangular" | custom-call | tf_op jit(solution)/shard_map/cholesky | solution.py:50
  398.5 2.3 convolution_subtract_fusion.2
  400.9 11.7 %cholesky.512 = f32[128,128]{1,0:T(8,128)S(1)} custom-call(f32[128,128]{1,0:T(8,128)S(1)} %cholesky.681), custom_call_target="Cholesky" | custom-call | tf_op jit(solution)/shard_map/cholesky | solution.py:50
  413.9 9.8 %custom-call.52 = f32[1,128,128]{1,2,0:T(8,128)S(1)} custom-call(f32[1,128,128]{2,1,0:T(8,128)S(1)} %get-tuple-element.45), custom_call_target="InvertDiagBlocksLowerTriangular" | custom-call | tf_op jit(solution)/shard_map/cholesky | solution.py:50
  424.8 2.3 convolution_subtract_fusion.3
  427.1 12.1 %cholesky.531 = f32[128,128]{1,0:T(8,128)S(1)} custom-call(f32[128,128]{1,0:T(8,128)S(1)} %cholesky.686), custom_call_target="Cholesky" | custom-call | tf_op jit(solution)/shard_map/cholesky | solution.py:50
  440.5 9.8 %custom-call.53 = f32[1,128,128]{1,2,0:T(8,128)S(1)} custom-call(f32[1,128,128]{2,1,0:T(8,128)S(1)} %get-tuple-element.42), custom_call_target="InvertDiagBlocksLowerTriangular" | custom-call | tf_op jit(solution)/shard_map/cholesky | solution.py:50
  451.3 2.3 convolution_subtract_fusion.4
  453.6 11.7 %cholesky.551 = f32[128,128]{1,0:T(8,128)S(1)} custom-call(f32[128,128]{1,0:T(8,128)S(1)} %cholesky.691), custom_call_target="Cholesky" | custom-call | tf_op jit(solution)/shard_map/cholesky | solution.py:50
  466.7 9.8 %custom-call.54 = f32[1,128,128]{1,2,0:T(8,128)S(1)} custom-call(f32[1,128,128]{2,1,0:T(8,128)S(1)} %get-tuple-element.39), custom_call_target="InvertDiagBlocksLowerTriangular" | custom-call | tf_op jit(solution)/shard_map/cholesky | solution.py:50
  477.4 2.0 convolution_subtract_fusion.5
  479.5 11.9 %cholesky.571 = f32[128,128]{1,0:T(8,128)S(1)} custom-call(f32[128,128]{1,0:T(8,128)S(1)} %cholesky.696), custom_call_target="Cholesky" | custom-call | tf_op jit(solution)/shard_map/cholesky | solution.py:50
  492.6 9.8 %custom-call.55 = f32[1,128,128]{1,2,0:T(8,128)S(1)} custom-call(f32[1,128,128]{2,1,0:T(8,128)S(1)} %get-tuple-element.36), custom_call_target="InvertDiagBlocksLowerTriangular" | custom-call | tf_op jit(solution)/shard_map/cholesky | solution.py:50
  503.3 1.8 convolution_subtract_fusion.6
  505.1 11.7 %cholesky.589 = f32[128,128]{1,0:T(8,128)S(1)} custom-call(f32[128,128]{1,0:T(8,128)S(1)} %convolution_subtract_fusion.6), custom_call_target="Cholesky" | custom-call | tf_op jit(solution)/shard_map/cholesky | solution.py:50
  523.1 4.8 select_bitcast_fusion
  527.9 5.3 copy.41
  (91 shorter events, 42.4 us)
Async XLA Ops:
  7.2 240.8 %copy-start = (f32[1024,128]{1,0:T(8,128)S(1)}, f32[1024,128]{1,0:T(8,128)}, u32[]{:S(2)}) copy-start(f32[1024,128]{1,0:T(8,128)} %param.10) | copy-start | bytes 1572868
  7.2 5.9 %copy-start.3 = (s32[8,128]{1,0:T(8,128)S(1)}, s32[8,128]{1,0:T(8,128)}, u32[]{:S(2)}) copy-start(s32[8,128]{1,0:T(8,128)} %constant.336.clone.1) | copy-start | bytes 12292
  7.2 5.2 copy-start.2
  7.2 30.6 %all-to-all-start = ((bf16[4,1024,256]{2,1,0:T(8,128)(2,1)}), bf16[4,1024,256]{2,1,0:T(8,128)(2,1)S(1)}, u32[]{:S(2)}, u32[]{:S(2)}) async-start(bf16[4,1024,256]{2,1,0:T(8,128)(2,1)} %bitcast.129), calls=%async_computation | async-start | bytes 4194304 | tf_op jit(solution)/shard_map/all_to_all | solution.py:40
  12.4 191.9 %all-reduce.10.cloned.1.call-start = ((), (), s32[]{:S(2)}) async-start(), calls=%async_computation.1 | async-start | bytes 4718592 | tf_op jit(solution)/shard_map/psum | solution.py:47
  204.3 5.7 %slice-start = ((f32[128,4608]{0,1:T(8,128)}), f32[128,640]{0,1:T(8,128)S(1)}, s32[]{:S(2)}) async-start(f32[128,4608]{0,1:T(8,128)} %all-reduce.10.cloned.1.call-done), calls=%async_computation.2 | async-start | bytes 655360 | tf_op jit(solution)/shard_map/slice | solution.py:30
  204.3 6.6 %slice-start.1 = ((f32[128,4608]{0,1:T(8,128)}), f32[128,512]{0,1:T(8,128)S(1)}, s32[]{:S(2)}) async-start(f32[128,4608]{0,1:T(8,128)} %all-reduce.10.cloned.1.call-done), calls=%async_computation.3 | async-start | bytes 524288 | tf_op jit(solution)/shard_map/slice | solution.py:30
  204.3 7.4 %slice-start.2 = ((f32[128,4608]{0,1:T(8,128)}), f32[128,384]{0,1:T(8,128)S(1)}, s32[]{:S(2)}) async-start(f32[128,4608]{0,1:T(8,128)} %all-reduce.10.cloned.1.call-done), calls=%async_computation.4 | async-start | bytes 393216 | tf_op jit(solution)/shard_map/slice | solution.py:30
  205.4 7.1 %slice-start.3 = ((f32[128,4608]{0,1:T(8,128)}), f32[128,256]{0,1:T(8,128)S(1)}, s32[]{:S(2)}) async-start(f32[128,4608]{0,1:T(8,128)} %all-reduce.10.cloned.1.call-done), calls=%async_computation.5 | async-start | bytes 262144 | tf_op jit(solution)/shard_map/slice | solution.py:30
  205.4 7.9 %slice-start.4 = ((f32[128,4608]{0,1:T(8,128)}), f32[128,128]{0,1:T(8,128)S(1)}, s32[]{:S(2)}) async-start(f32[128,4608]{0,1:T(8,128)} %all-reduce.10.cloned.1.call-done), calls=%async_computation.6 | async-start | bytes 131072 | tf_op jit(solution)/shard_map/slice | solution.py:30
  223.7 2.0 copy-start.1
Sparse Core Ops, SparseCore 0:
  51.6 152.6 all-reduce.9
where the time goes:
time: 549 us; the launch traced here: 540 us
  other arithmetic  263 us (48%)
  waiting for transfers between devices  167 us (30%)
  matrix products  57.1 us (10%)
  local copies, waits for them, and re-layouts  28.4 us (5%)
  between operations  19.6 us (4%)
    another operation x31, other arithmetic, body(): upper_factor = lax.linalg.cholesky(shifted, symmetrize_input=False).T  173 us
    psum x1, waiting for transfers between devices, body(): packed = lax.psum(pack_upper(masked), ('dof', 'snap'))  153 us
    another operation x9, other arithmetic, body(): lower_factor = jnp.linalg.cholesky(correlation)  37.2 us
    another operation x6, other arithmetic, body(): lax.linalg.triangular_solve(lower_factor, image, left_side=False, lower=T...  31.4 us
    another operation x14, matrix products, body(): upper_factor = lax.linalg.cholesky(shifted, symmetrize_input=False).T  23.1 us
    dot_general x3, matrix products, body(): jnp.dot(shifted, subspace, precision=lax.Precision.HIGHEST, preferred_ele...  16.4 us
    all_to_all x1, waiting for transfers between devices, body(): rows = lax.all_to_all(snapshots, 'snap', 0, 1, tiled=True)  14.4 us
    unnamed x16, local copies, waits for them, and re-layouts  14.2 us
  transfers between devices with their start and end apart: 2, of which 2 were waited for; matrix products, arithmetic and copies ran while one was open for 2% of the time, Pallas kernels for 0%

commit v1 on v0

--- a/solution.py
+++ b/solution.py
@@ -7,6 +7,18 @@
 ITERS = 3
 PASSES = 16
 TILE = 128
+
+
+def cut_along(array, dim, size):
+    dims = array.shape
+    blocks = array.reshape(*dims[:dim], size, dims[dim] // size, *dims[dim + 1 :])
+    return jnp.moveaxis(blocks, dim, 0)
+
+
+def joined_along(blocks, dim):
+    blocks = jnp.moveaxis(blocks, 0, dim)
+    shape = blocks.shape
+    return blocks.reshape(*shape[:dim], shape[dim] * shape[dim + 1], *shape[dim + 2 :])
 
 
 def pack_upper(rows):
@@ -37,7 +49,14 @@
 
 
 def body(snapshots, lengths, start_block):
-    rows = lax.all_to_all(snapshots, "snap", 0, 1, tiled=True)
+    size, index = (lax.axis_size("snap"), lax.axis_index("snap"))
+    blocks_2 = cut_along(snapshots, 0, size)
+    finished = [blocks_2[index]]
+    for step in range(1, size):
+        sent = blocks_2[index ^ step]
+        finished.append(lax.ppermute(sent, "snap", [(i_2, i_2 ^ step) for i_2 in range(size)]))
+    blocks_2 = jnp.stack(finished)[index ^ jnp.arange(size)]
+    rows = joined_along(blocks_2, 1)
     width = rows.shape[1]
     col_length = jnp.repeat(lengths, STEPS, total_repeat_length=width)
     columns = jnp.arange(width, dtype=jnp.int32)

time: 549 us -> 554 us (level)
    all_to_all x1 -> x0, waiting for transfers between devices: 14.4 us -> none  [body(): rows = lax.all_to_all(snapshots, 'snap', 0, 1, tiled=True)]
    ppermute x0 -> x3, waiting for transfers between devices: none -> 11.5 us  [body(): lax.ppermute(sent, 'snap', [(i_2, i_2 ^ step) for i_2 in range(size)])]
  transfers between devices with their start and end apart: 2 -> 4, of which waited for: 2 -> 3; matrix products, arithmetic and copies ran while one was open for 2% -> 2% of each run, Pallas kernels for 0% -> 0%
where the time goes in v1:
time: 554 us; the launch traced here: 544 us
  other arithmetic  263 us (47%)
  waiting for transfers between devices  166 us (30%)
  matrix products  57.1 us (10%)
  local copies, waits for them, and re-layouts  33.7 us (6%)
  between operations  19.7 us (4%)
    another operation x31, other arithmetic, body(): upper_factor = lax.linalg.cholesky(shifted, symmetrize_input=False).T  173 us
    psum x1, waiting for transfers between devices, body(): packed = lax.psum(pack_upper(masked), ('dof', 'snap'))  154 us
    another operation x9, other arithmetic, body(): lower_factor = jnp.linalg.cholesky(correlation)  37.2 us
    another operation x6, other arithmetic, body(): lax.linalg.triangular_solve(lower_factor, image, left_side=False, lower=T...  31.4 us
    another operation x14, matrix products, body(): upper_factor = lax.linalg.cholesky(shifted, symmetrize_input=False).T  23.2 us
    dot_general x3, matrix products, body(): jnp.dot(shifted, subspace, precision=lax.Precision.HIGHEST, preferred_ele...  16.4 us
    unnamed x16, local copies, waits for them, and re-layouts  14.2 us
    ppermute x3, waiting for transfers between devices, body(): lax.ppermute(sent, 'snap', [(i_2, i_2 ^ step) for i_2 in range(size)])  11.5 us
  transfers between devices with their start and end apart: 4, of which 3 were waited for; matrix products, arithmetic and copies ran while one was open for 2% of the time, Pallas kernels for 0%

profile of v1, /device:TPU:1, one launch (start us, length us, event | category | flops | bytes accessed | tf_op | source)
XLA Modules:
  0.0 543.8 jit_solution(17604062609772087967)
XLA Ops:
  7.3 1.7 constant_dynamic-slice_fusion
  9.0 3.6 collective-permute-start.2
  14.1 4.4 compare_select_fusion.1
  18.6 5.7 %fusion.98 = pred[1024]{0:T(1024)(128)(4,1)S(1)} fusion(pred[1024]{0:T(1024)(128)(4,1)S(1)} %get-tuple-element.30, pred[1024]{0:T(1024)(128)(4,1)S(1)} %get-tuple-element.29, pred[1024]{0:T(1024)(128)(4,1)S(1)} %get-tuple-element.28, pred[1024]{0:T(1024)(128)(4,1)S(1)} %get-tuple-element.27, pred[1024]{0:T(1024)(128)(4,1)S(1)} %get-tuple-element.26, ...), kind=kLoop, calls=%fused_computation.164 | loop fusion | flops 25600 | bytes 18500 | tf_op jit(solution)/shard_map/lt | solution.py:63
  24.3 11.0 %collective-permute-done.2 = bf16[1024,256]{1,0:T(8,128)(2,1)S(1)} collective-permute-done((bf16[1024,256]{1,0:T(8,128)(2,1)S(1)}, bf16[1024,256]{1,0:T(8,128)(2,1)S(1)}, u32[]{:S(2)}, u32[]{:S(2)}) %collective-permute-start.2) | collective-permute-done | bytes 524320 | tf_op jit(solution)/shard_map/ppermute | solution.py:57
  36.1 2.0 gather_fusion
  38.1 4.0 copy.29
  42.1 1.8 bitcast_select_fusion.1
  53.5 154.3 %all-reduce.10.cloned.1.call-done = f32[128,4608]{0,1:T(8,128)} async-done(((f32[128,4608]{0,1:T(8,128)}), f32[128,4608]{0,1:T(8,128)}) %all-reduce.10.cloned.1.call-update) | async-done | bytes 2359312 | tf_op jit(solution)/shard_map/psum | solution.py:66
  208.9 1.9 slice_dynamic-update-slice_fusion
  217.7 5.3 copy.37
  223.0 4.2 fusion.1
  227.2 2.0 copy-done.1
  229.2 11.7 %cholesky.247 = f32[128,128]{1,0:T(8,128)S(1)} custom-call(f32[128,128]{1,0:T(8,128)S(1)} %cholesky.667), custom_call_target="Cholesky" | custom-call | tf_op jit(solution)/shard_map/cholesky | solution.py:69
  241.6 9.8 %custom-call.49 = f32[1,128,128]{1,2,0:T(8,128)S(1)} custom-call(f32[1,128,128]{2,1,0:T(8,128)S(1)} %get-tuple-element.58), custom_call_target="InvertDiagBlocksLowerTriangular" | custom-call | tf_op jit(solution)/shard_map/cholesky | solution.py:69
  251.4 5.4 fusion.107
  258.0 11.7 %cholesky.636 = f32[128,128]{1,0:T(8,128)S(1)} custom-call(f32[128,128]{1,0:T(8,128)S(1)} %fusion.63), custom_call_target="Cholesky" | custom-call | tf_op jit(solution)/shard_map/jit(cholesky)/cholesky | solution.py:83
  271.0 9.8 %custom-call.58 = f32[1,128,128]{1,2,0:T(8,128)S(1)} custom-call(f32[1,128,128]{2,1,0:T(8,128)S(1)} %fusion.46), custom_call_target="InvertDiagBlocksLowerTriangular" | custom-call | tf_op jit(solution)/shard_map/triangular_solve/custom-call.16 | solution.py:84
  281.5 5.4 %fusion.109 = f32[1024,128]{1,0:T(8,128)S(1)} fusion(f32[1024,1024]{1,0:T(8,128)} %copy-done.1, f32[1024,128]{0,1:T(8,128)S(1)} %convolution_bitcast_fusion.2), kind=kOutput, calls=%fused_computation.201 | convolution fusion | flops 1610612736 | bytes 5242880 | tf_op jit(solution)/shard_map/dot_general | solution.py:73
  288.1 11.7 %cholesky.647 = f32[128,128]{1,0:T(8,128)S(1)} custom-call(f32[128,128]{1,0:T(8,128)S(1)} %fusion.61), custom_call_target="Cholesky" | custom-call | tf_op jit(solution)/shard_map/jit(cholesky)/cholesky | solution.py:83
  301.1 9.8 %custom-call.59 = f32[1,128,128]{1,2,0:T(8,128)S(1)} custom-call(f32[1,128,128]{2,1,0:T(8,128)S(1)} %fusion.47), custom_call_target="InvertDiagBlocksLowerTriangular" | custom-call | tf_op jit(solution)/shard_map/triangular_solve/custom-call.16 | solution.py:84
  311.6 5.6 %fusion.111 = f32[1024,128]{1,0:T(8,128)S(1)} fusion(f32[1024,1024]{1,0:T(8,128)} %copy-done.1, f32[1024,128]{0,1:T(8,128)S(1)} %convolution_bitcast_fusion.1), kind=kOutput, calls=%fused_computation.203 | convolution fusion | flops 1610612736 | bytes 5242880 | tf_op jit(solution)/shard_map/dot_general | solution.py:73
  318.3 11.7 %cholesky.658 = f32[128,128]{1,0:T(8,128)S(1)} custom-call(f32[128,128]{1,0:T(8,128)S(1)} %fusion.59), custom_call_target="Cholesky" | custom-call | tf_op jit(solution)/shard_map/jit(cholesky)/cholesky | solution.py:83
  331.4 9.8 %custom-call.60 = f32[1,128,128]{1,2,0:T(8,128)S(1)} custom-call(f32[1,128,128]{2,1,0:T(8,128)S(1)} %fusion.48), custom_call_target="InvertDiagBlocksLowerTriangular" | custom-call | tf_op jit(solution)/shard_map/triangular_solve/custom-call.16 | solution.py:84
  341.9 3.1 fusion.113
  345.0 2.5 cholesky.279
  347.4 2.4 constant_dynamic-update-slice_fusion
  351.4 11.9 %cholesky.270 = f32[128,128]{1,0:T(8,128)S(1)} custom-call(f32[128,128]{1,0:T(8,128)S(1)} %cholesky.671), custom_call_target="Cholesky" | custom-call | tf_op jit(solution)/shard_map/cholesky | solution.py:69
  364.6 9.8 %custom-call.50 = f32[1,128,128]{1,2,0:T(8,128)S(1)} custom-call(f32[1,128,128]{2,1,0:T(8,128)S(1)} %get-tuple-element.55), custom_call_target="InvertDiagBlocksLowerTriangular" | custom-call | tf_op jit(solution)/shard_map/cholesky | solution.py:69
  375.7 2.1 convolution_subtract_fusion.1
  377.8 11.7 %cholesky.493 = f32[128,128]{1,0:T(8,128)S(1)} custom-call(f32[128,128]{1,0:T(8,128)S(1)} %cholesky.676), custom_call_target="Cholesky" | custom-call | tf_op jit(solution)/shard_map/cholesky | solution.py:69
  390.9 10.0 %custom-call.51 = f32[1,128,128]{1,2,0:T(8,128)S(1)} custom-call(f32[1,128,128]{2,1,0:T(8,128)S(1)} %get-tuple-element.52), custom_call_target="InvertDiagBlocksLowerTriangular" | custom-call | tf_op jit(solution)/shard_map/cholesky | solution.py:69
  402.1 2.3 convolution_subtract_fusion.2
  404.4 11.7 %cholesky.512 = f32[128,128]{1,0:T(8,128)S(1)} custom-call(f32[128,128]{1,0:T(8,128)S(1)} %cholesky.681), custom_call_target="Cholesky" | custom-call | tf_op jit(solution)/shard_map/cholesky | solution.py:69
  417.4 9.8 %custom-call.52 = f32[1,128,128]{1,2,0:T(8,128)S(1)} custom-call(f32[1,128,128]{2,1,0:T(8,128)S(1)} %get-tuple-element.49), custom_call_target="InvertDiagBlocksLowerTriangular" | custom-call | tf_op jit(solution)/shard_map/cholesky | solution.py:69
  428.3 2.3 convolution_subtract_fusion.3
  430.6 12.1 %cholesky.531 = f32[128,128]{1,0:T(8,128)S(1)} custom-call(f32[128,128]{1,0:T(8,128)S(1)} %cholesky.686), custom_call_target="Cholesky" | custom-call | tf_op jit(solution)/shard_map/cholesky | solution.py:69
  444.0 9.8 %custom-call.53 = f32[1,128,128]{1,2,0:T(8,128)S(1)} custom-call(f32[1,128,128]{2,1,0:T(8,128)S(1)} %get-tuple-element.46), custom_call_target="InvertDiagBlocksLowerTriangular" | custom-call | tf_op jit(solution)/shard_map/cholesky | solution.py:69
  454.8 2.3 convolution_subtract_fusion.4
  457.1 11.7 %cholesky.551 = f32[128,128]{1,0:T(8,128)S(1)} custom-call(f32[128,128]{1,0:T(8,128)S(1)} %cholesky.691), custom_call_target="Cholesky" | custom-call | tf_op jit(solution)/shard_map/cholesky | solution.py:69
  470.2 9.8 %custom-call.54 = f32[1,128,128]{1,2,0:T(8,128)S(1)} custom-call(f32[1,128,128]{2,1,0:T(8,128)S(1)} %get-tuple-element.43), custom_call_target="InvertDiagBlocksLowerTriangular" | custom-call | tf_op jit(solution)/shard_map/cholesky | solution.py:69
  480.9 2.0 convolution_subtract_fusion.5
  483.0 11.9 %cholesky.571 = f32[128,128]{1,0:T(8,128)S(1)} custom-call(f32[128,128]{1,0:T(8,128)S(1)} %cholesky.696), custom_call_target="Cholesky" | custom-call | tf_op jit(solution)/shard_map/cholesky | solution.py:69
  496.2 9.8 %custom-call.55 = f32[1,128,128]{1,2,0:T(8,128)S(1)} custom-call(f32[1,128,128]{2,1,0:T(8,128)S(1)} %get-tuple-element.40), custom_call_target="InvertDiagBlocksLowerTriangular" | custom-call | tf_op jit(solution)/shard_map/cholesky | solution.py:69
  506.8 1.8 convolution_subtract_fusion.6
  508.6 11.7 %cholesky.589 = f32[128,128]{1,0:T(8,128)S(1)} custom-call(f32[128,128]{1,0:T(8,128)S(1)} %convolution_subtract_fusion.6), custom_call_target="Cholesky" | custom-call | tf_op jit(solution)/shard_map/cholesky | solution.py:69
  526.6 4.8 select_bitcast_fusion
  531.4 5.3 copy.41
  (100 shorter events, 46.9 us)
Async XLA Ops:
  7.2 244.3 %copy-start = (f32[1024,128]{1,0:T(8,128)S(1)}, f32[1024,128]{1,0:T(8,128)}, u32[]{:S(2)}) copy-start(f32[1024,128]{1,0:T(8,128)} %param.10) | copy-start | bytes 1572868
  7.2 6.8 %copy-start.3 = (s32[8,128]{1,0:T(8,128)S(1)}, s32[8,128]{1,0:T(8,128)}, u32[]{:S(2)}) copy-start(s32[8,128]{1,0:T(8,128)} %constant.345.clone.1) | copy-start | bytes 12292
  7.2 6.1 %copy-start.2 = (s32[16]{0:T(128)S(1)}, s32[16]{0:T(128)}, u32[]{:S(2)}) copy-start(s32[16]{0:T(128)} %param.9) | copy-start | bytes 196
  7.2 200.6 %all-reduce.10.cloned.1.call-start = ((), (), s32[]{:S(2)}) async-start(), calls=%async_computation | async-start | bytes 4718592 | tf_op jit(solution)/shard_map/psum | solution.py:66
  9.0 26.4 %collective-permute-start.2 = (bf16[1024,256]{1,0:T(8,128)(2,1)S(1)}, bf16[1024,256]{1,0:T(8,128)(2,1)S(1)}, u32[]{:S(2)}, u32[]{:S(2)}) collective-permute-start(bf16[1024,256]{1,0:T(8,128)(2,1)S(1)} %get-tuple-element.34), channel_id=1, source_target_pairs={{0,3},{1,2},{2,1},{3,0},{4,7},{5,6},{6,5},{7,4},{8,11},{9,10},{10,... | collective-permute-start | bytes 1572872 | tf_op jit(solution)/shard_map/ppermute | solution.py:57
  12.6 22.7 %collective-permute-start.1 = (bf16[1024,256]{1,0:T(8,128)(2,1)S(1)}, bf16[1024,256]{1,0:T(8,128)(2,1)S(1)}, u32[]{:S(2)}, u32[]{:S(2)}) collective-permute-start(bf16[1024,256]{1,0:T(8,128)(2,1)S(1)} %get-tuple-element.35), channel_id=1, source_target_pairs={{0,2},{1,3},{2,0},{3,1},{4,6},{5,7},{6,4},{7,5},{8,10},{9,11},{10,... | collective-permute-start | bytes 1572872 | tf_op jit(solution)/shard_map/ppermute | solution.py:57
  13.0 22.9 %collective-permute-start = (bf16[1024,256]{1,0:T(8,128)(2,1)S(1)}, bf16[1024,256]{1,0:T(8,128)(2,1)S(1)}, u32[]{:S(2)}, u32[]{:S(2)}) collective-permute-start(bf16[1024,256]{1,0:T(8,128)(2,1)S(1)} %get-tuple-element.36), channel_id=1, source_target_pairs={{0,1},{1,0},{2,3},{3,2},{4,5},{5,4},{6,7},{7,6},{8,9},{9,8},{10,11... | collective-permute-start | bytes 1572872 | tf_op jit(solution)/shard_map/ppermute | solution.py:57
  207.8 5.7 %slice-start = ((f32[128,4608]{0,1:T(8,128)}), f32[128,640]{0,1:T(8,128)S(1)}, s32[]{:S(2)}) async-start(f32[128,4608]{0,1:T(8,128)} %all-reduce.10.cloned.1.call-done), calls=%async_computation.1 | async-start | bytes 655360 | tf_op jit(solution)/shard_map/slice | solution.py:42
  207.8 6.6 %slice-start.1 = ((f32[128,4608]{0,1:T(8,128)}), f32[128,512]{0,1:T(8,128)S(1)}, s32[]{:S(2)}) async-start(f32[128,4608]{0,1:T(8,128)} %all-reduce.10.cloned.1.call-done), calls=%async_computation.2 | async-start | bytes 524288 | tf_op jit(solution)/shard_map/slice | solution.py:42
  207.8 7.4 %slice-start.2 = ((f32[128,4608]{0,1:T(8,128)}), f32[128,384]{0,1:T(8,128)S(1)}, s32[]{:S(2)}) async-start(f32[128,4608]{0,1:T(8,128)} %all-reduce.10.cloned.1.call-done), calls=%async_computation.3 | async-start | bytes 393216 | tf_op jit(solution)/shard_map/slice | solution.py:42
  208.9 7.1 %slice-start.3 = ((f32[128,4608]{0,1:T(8,128)}), f32[128,256]{0,1:T(8,128)S(1)}, s32[]{:S(2)}) async-start(f32[128,4608]{0,1:T(8,128)} %all-reduce.10.cloned.1.call-done), calls=%async_computation.4 | async-start | bytes 262144 | tf_op jit(solution)/shard_map/slice | solution.py:42
  208.9 7.9 %slice-start.4 = ((f32[128,4608]{0,1:T(8,128)}), f32[128,128]{0,1:T(8,128)S(1)}, s32[]{:S(2)}) async-start(f32[128,4608]{0,1:T(8,128)} %all-reduce.10.cloned.1.call-done), calls=%async_computation.5 | async-start | bytes 131072 | tf_op jit(solution)/shard_map/slice | solution.py:42
  227.2 2.0 copy-start.1
Sparse Core Ops, SparseCore 0:
  53.6 154.1 all-reduce.9
